TPU v7x, 512 devices: a whole 4x4x16 slice. The times are simulated.
512 devices in a mesh: seq: 16 (over z), exp: 32 (over x, y, core).
Axes of the slice: x: 4, y: 4, z: 16, core: 2. Of those that a mesh axis runs over, the one named last changes fastest.
Arguments:
- queries: bfloat16 [2048, 8192], P('seq', 'exp'), may hold values from -6 to 6
- key_matrix: bfloat16 [2048, 8192], P('seq', 'exp'), may hold values from -6 to 6
- values: bfloat16 [2048, 8192], P('seq', 'exp'), may hold values from -6 to 6
- log_decay: float32 [64, 2048], P('exp', 'seq'), may hold values from -3 to 0
- residual: bfloat16 [2048, 3072], P('seq'), may hold values from -6 to 6
- out_weight: bfloat16 [3072, 8192], P('seq', 'exp'), may hold values from -0.0625 to 0.0625
- router: bfloat16 [3072, 32], replicated, may hold values from -0.109375 to 0.109375
- expert_ids: int32 [2048, 2], P('seq'), may hold values from 0 to 31, all different within a row; in each aligned block of 128 rows (0 to 127, 128 to 255, ...) at most 12 rows name the same one
- up_weight: bfloat16 [32, 3072, 4608], P('exp', None, 'seq'), may hold values from -0.109375 to 0.109375
- down_weight: bfloat16 [32, 4608, 3072], P('exp', 'seq'), may hold values from -0.09375 to 0.09375
Outputs:
- layer_out: bfloat16 [2048, 3072], P(('seq', 'exp'))
Inputs may be any that keep to these rules, and one draw needn't show every extreme that they name: `expert_ids`: in each aligned block of 128 rows (one sequence block) no expert is named by more than 12 rows, a bound that some block reaches; a row names 2 different experts.
All inputs are finite; a program needn't handle non-finite values.
Results may differ from a plain program's by a relative error of at most 0.015.
Values may be sent and summed in bfloat16 or wider, within the bound.
No kernel may reach another device: no remote copies, remote signals or barrier semaphores. Data moves between devices by JAX's collectives and lax.ppermute only.
A program may use at most 64 MiB of HBM per device.

v0:
```python
import jax
import jax.numpy as jnp
from jax import lax
from jax.sharding import PartitionSpec as P


def prefix(x, axis, combine, identity):
    length, index = (lax.axis_size(axis), lax.axis_index(axis))
    everything = jax.tree.map(
        lambda part, kind: lax.all_gather(part.astype(kind), axis), x, (jnp.bfloat16, jnp.bfloat16)
    )
    start = jax.tree.map(
        lambda part, zero: jnp.broadcast_to(jnp.asarray(zero, part.dtype), part.shape), x, identity
    )

    def turn(k, before):
        reached = k < index
        new = combine(
            before, jax.tree.map(lambda part, own: part[k].astype(own.dtype), everything, x)
        )
        return jax.tree.map(lambda a, b: jnp.where(reached, a, b), new, before)

    return lax.fori_loop(0, length, turn, start)


def compose(earlier, later):
    return (earlier[0] * later[0], later[0][:, None, None] * earlier[1] + later[1])


def shards(
    queries,
    key_matrix,
    values,
    log_decay,
    residual,
    out_weight,
    router,
    expert_ids,
    up_weight,
    down_weight,
):
    rows = queries.shape[0]
    heads_here = log_decay.shape[0]
    width = queries.shape[1] // heads_here

    def split_heads(array):
        return array.astype(jnp.float32).reshape(rows, heads_here, width).transpose(1, 0, 2)

    qloc = split_heads(queries)
    kloc = split_heads(key_matrix)
    vloc = split_heads(values)
    cum = jnp.cumsum(log_decay, axis=1)
    last = cum[:, -1:]
    carry_decay = jnp.exp(last[:, 0])
    kscaled = kloc * jnp.exp(last - cum)[:, :, None]
    local_state = jnp.einsum("hjd,hje->hde", kscaled, vloc, precision=lax.Precision.HIGHEST)
    empty = jnp.zeros((heads_here, width, width), jnp.float32)
    _, state_in = prefix(
        (carry_decay, local_state), "seq", compose, (jnp.ones_like(carry_decay), empty)
    )
    lower = jnp.arange(rows)[:, None] >= jnp.arange(rows)[None, :]
    diff = cum[:, :, None] - cum[:, None, :]
    weight = jnp.where(lower[None], jnp.exp(jnp.where(lower[None], diff, 0.0)), 0.0)
    scores = jnp.einsum("hid,hjd->hij", qloc, kloc, precision=lax.Precision.HIGHEST) * weight
    inner = jnp.einsum("hij,hjd->hid", scores, vloc, precision=lax.Precision.HIGHEST)
    outer = jnp.exp(cum)[:, :, None] * jnp.einsum(
        "hid,hde->hie", qloc, state_in, precision=lax.Precision.HIGHEST
    )
    mixed = inner + outer
    mixed = mixed * lax.rsqrt(jnp.mean(mixed * mixed, axis=-1, keepdims=True) + 1e-06)
    attn = mixed.transpose(1, 0, 2).reshape(rows, heads_here * width).astype(jnp.bfloat16)
    stream = residual.astype(jnp.float32)
    normed = (stream * lax.rsqrt(jnp.mean(stream * stream, axis=-1, keepdims=True) + 1e-05)).astype(
        jnp.bfloat16
    )
    logits = jnp.dot(normed, router, preferred_element_type=jnp.float32)
    count_experts = router.shape[1]
    select_experts = (
        expert_ids[:, :, None] == jnp.arange(count_experts, dtype=jnp.int32)[None, None, :]
    )
    chosen = jnp.sum(jnp.where(select_experts, logits[:, None, :], 0.0), axis=-1)
    score = jax.nn.sigmoid(chosen)
    gates = score / jnp.sum(score, axis=1, keepdims=True)
    topk = expert_ids.shape[1]
    owner = lax.axis_index("exp")
    capacity = 3 * rows * topk // (2 * lax.axis_size("exp"))
    mine = (expert_ids.reshape(-1) == owner).astype(jnp.int32)
    ranks = jnp.cumsum(mine) - mine
    slot_pick = (ranks[None, :] == jnp.arange(capacity, dtype=jnp.int32)[:, None]) & (
        mine[None, :] == 1
    )
    slot_pick = slot_pick.astype(jnp.float32).reshape(capacity, rows, topk)
    token_pick = jnp.sum(slot_pick, axis=2).astype(jnp.bfloat16)
    slot_rows = jnp.dot(token_pick, normed, preferred_element_type=jnp.float32).astype(jnp.bfloat16)
    gathered_rows, full_weight = (
        lax.all_gather(slot_rows, "seq", axis=0, tiled=True),
        lax.all_gather(out_weight, "seq", axis=0, tiled=True),
    )
    projected = lax.dot_general(
        attn, full_weight, (((1,), (1,)), ((), ())), preferred_element_type=jnp.float32
    )
    hidden = jax.nn.silu(
        jnp.dot(gathered_rows, up_weight[0], preferred_element_type=jnp.float32)
    ).astype(jnp.bfloat16)
    expert_out = lax.psum_scatter(
        jnp.dot(hidden, down_weight[0], preferred_element_type=jnp.float32).astype(jnp.bfloat16),
        "seq",
        scatter_dimension=0,
        tiled=True,
    ).astype(jnp.float32)
    combine = jnp.einsum("cbk,bk->bc", slot_pick, gates, precision=lax.Precision.HIGHEST)
    contribution = jnp.dot(combine, expert_out, precision=lax.Precision.HIGHEST)
    summed = lax.psum_scatter(
        (projected + contribution).astype(jnp.bfloat16), "exp", scatter_dimension=0, tiled=True
    ).astype(jnp.float32)
    own_rows = summed.shape[0]
    own = lax.dynamic_slice_in_dim(stream, owner * own_rows, own_rows, 0)
    return (own + summed).astype(jnp.bfloat16)


def solution(mesh):
    in_specs = (
        P("seq", "exp"),
        P("seq", "exp"),
        P("seq", "exp"),
        P("exp", "seq"),
        P("seq", None),
        P("seq", "exp"),
        P(),
        P("seq", None),
        P("exp", None, "seq"),
        P("exp", "seq", None),
    )
    out_specs = P(("seq", "exp"), None)
    return jax.shard_map(shards, mesh=mesh, in_specs=in_specs, out_specs=out_specs, check_vma=False)
```

profile of v0, /device:TPU:1, one launch (start us, length us, event | category | flops | bytes accessed | tf_op | source)
XLA Modules:
  0.0 382.8 jit_solution(2274321475533020910)
XLA Ops:
  6.6 1.2 reduce_window_sum.27
  8.0 1.0 copy.68
  9.0 1.7 convolution_convert_fusion.2
  12.6 1.4 multiply_reduce_fusion
  14.0 1.0 fusion.3
  17.5 30.4 %all-reduce = bf16[32]{0:T(256)(128)(2,1)S(1)} all-reduce(bf16[32]{0:T(256)(128)(2,1)S(1)} %dynamic-update-slice), channel_id=2, replica_groups=mesh['seq'=16,'exp'=32] {'seq'}, use_global_device_ids=true, to_apply=%add | all-reduce | flops 32 | bytes 128
  49.4 26.7 %all-gather.9.cloned.1.call-done = bf16[32,128,128]{2,1,0:T(8,128)(2,1)} async-done(((bf16[2,128,128]{2,1,0:T(8,128)(2,1)}), bf16[32,128,128]{2,1,0:T(8,128)(2,1)}) %all-gather.9.cloned.1.call-update) | async-done | bytes 1048592 | tf_op jit(solution)/shard_map/all_gather | solution.py:10
  76.1 15.5 %while.14 = (s32[]{:T(128)}, f32[2,128,128]{2,1,0:T(8,128)S(1)}, s32[]{:T(128)}, bf16[16,2]{1,0:T(8,128)(2,1)S(1)}, bf16[16,2,128,128]{3,2,1,0:T(8,128)(2,1)}, /*index=5*/s32[]{:T(128)}, s32[]{:T(128)}) while((s32[]{:T(128)}, f32[2,128,128]{2,1,0:T(8,128)S(1)}, s32[]{:T(128)}, bf16[16,2]{1,0:T(8,128)(2,1)S(1)}, ...), condition=%wide.region_2.3_spmd.clone, body=%wide.region_1.2_spmd.clone.sunk | while | flops 163846 | bytes 327805 | solution.py:23
  78.1 0.9 fusion.49
  79.1 0.9 fusion.49
  81.0 0.9 fusion.49
  82.9 0.9 fusion.49
  83.9 0.9 fusion.49
  85.9 0.9 fusion.49
  86.8 0.9 fusion.49
  92.3 55.7 %all-gather.11.cloned.1.call-done = bf16[16,12,3072]{2,1,0:T(8,128)(2,1)} async-done(((bf16[1,12,3072]{2,1,0:T(8,128)(2,1)}), bf16[16,12,3072]{2,1,0:T(8,128)(2,1)}) %all-gather.11.cloned.1.call-update) | async-done | bytes 1179664 | tf_op jit(solution)/shard_map/all_gather | solution.py:96
  147.9 2.3 reshape.178
  150.2 4.7 %convolution_convert_fusion = bf16[192,3072]{1,0:T(8,128)(2,1)} fusion(bf16[1,288,3072]{2,1,0:T(8,128)(2,1)S(1)} %copy-done, bf16[192,3072]{1,0:T(8,128)(2,1)} %reshape.178, bf16[1,3072,288]{1,2,0:T(8,128)(2,1)} %param.20), kind=kOutput, calls=%fused_computation.3 | convolution fusion | flops 680343552 | bytes 5898240 | tf_op jit(solution)/shard_map/dot_general | solution.py:106
  154.9 35.1 %fusion = bf16[16,3072]{1,0:T(8,128)(2,1)S(1)} fusion(bf16[192,3072]{1,0:T(8,128)(2,1)} %convolution_convert_fusion), kind=kCustom, calls=%all-reduce-scatter | all-reduce-scatter fusion | flops 786433 | bytes 1280000
  190.1 1.3 collective-permute-start
  191.4 3.6 collective-permute-start.1
  195.0 4.1 %collective-permute-start.2 = (bf16[16,3072]{1,0:T(8,128)(2,1)S(1)}, bf16[16,3072]{1,0:T(8,128)(2,1)S(1)}, u32[]{:S(2)}, u32[]{:S(2)}) collective-permute-start(bf16[16,3072]{1,0:T(8,128)(2,1)S(1)} %fusion), channel_id=1, source_target_pairs={{0,96},{32,128},{64,160},{96,192},{128,224},{160,256},{192,288},{2... | collective-permute-start | bytes 294920
  199.2 3.1 collective-permute-start.3
  202.3 3.2 collective-permute-done.3
  206.2 1.9 concatenate
  208.1 16.1 %all-gather.7.cloned.1.call-done = bf16[3072,256]{1,0:T(8,128)(2,1)} async-done(((bf16[192,256]{1,0:T(8,128)(2,1)}), bf16[3072,256]{1,0:T(8,128)(2,1)}) %all-gather.7.cloned.1.call-update) | async-done | bytes 1572880 | tf_op jit(solution)/shard_map/all_gather | solution.py:97
  224.2 2.0 fusion.34
  226.3 1.8 fusion.2
  228.1 1.3 convert_element_type.97
  229.4 1.3 dynamic-slice.3
  231.3 143.4 %all-reduce.6.cloned.1.call-done = bf16[128,3072]{1,0:T(8,128)(2,1)} async-done(((bf16[128,3072]{1,0:T(8,128)(2,1)}), bf16[128,3072]{1,0:T(8,128)(2,1)}) %all-reduce.6.cloned.1.call-update) | async-done | bytes 786448
  374.7 1.5 add_convert_fusion
  (86 shorter events, 14.8 us)
Async XLA Ops:
  6.5 143.7 %copy-start = (bf16[1,288,3072]{2,1,0:T(8,128)(2,1)S(1)}, bf16[1,288,3072]{2,1,0:T(8,128)(2,1)}, u32[]{:S(2)}) copy-start(bf16[1,288,3072]{2,1,0:T(8,128)(2,1)} %param.21) | copy-start | bytes 5308420
  6.5 9.5 %copy-start.6 = (u32[512]{0:T(512)S(1)}, u32[512]{0:T(512)}, u32[]{:S(2)}) copy-start(u32[512]{0:T(512)} %constant.67) | copy-start | bytes 6148
  6.5 7.5 %copy-start.1 = (bf16[128,3072]{1,0:T(8,128)(2,1)S(1)}, bf16[128,3072]{1,0:T(8,128)(2,1)}, u32[]{:S(2)}) copy-start(bf16[128,3072]{1,0:T(8,128)(2,1)} %param.16) | copy-start | bytes 2359300
  6.5 41.4 %copy-start.7 = (bf16[3072,32]{0,1:T(8,128)(2,1)S(1)}, bf16[3072,32]{0,1:T(8,128)(2,1)}, u32[]{:S(2)}) copy-start(bf16[3072,32]{0,1:T(8,128)(2,1)} %param.18) | copy-start | bytes 589828
  6.5 69.6 %all-gather.9.cloned.1.call-start = ((), (), s32[]{:S(2)}) async-start(), calls=%async_computation.1 | async-start | bytes 1114112 | tf_op jit(solution)/shard_map/all_gather | solution.py:10
  10.7 137.3 %all-gather.11.cloned.1.call-start = ((), (), s32[]{:S(2)}) async-start(), calls=%async_computation.2 | async-start | bytes 1671168 | tf_op jit(solution)/shard_map/all_gather | solution.py:96
  12.2 36.2 %copy-start.5 = (s32[128,2]{0,1:T(2,128)S(1)}, s32[128,2]{0,1:T(2,128)}, u32[]{:S(2)}) copy-start(s32[128,2]{0,1:T(2,128)} %param.19) | copy-start | bytes 3076
  12.2 36.3 %copy-start.4 = (bf16[128,256]{1,0:T(8,128)(2,1)S(1)}, bf16[128,256]{1,0:T(8,128)(2,1)}, u32[]{:S(2)}) copy-start(bf16[128,256]{1,0:T(8,128)(2,1)} %param.12) | copy-start | bytes 196612
  15.0 209.2 %all-gather.7.cloned.1.call-start = ((), (), s32[]{:S(2)}) async-start(), calls=%async_computation | async-start | bytes 1671168 | tf_op jit(solution)/shard_map/all_gather | solution.py:97
  15.7 359.0 %all-reduce.6.cloned.1.call-start = ((), (), s32[]{:S(2)}) async-start(), calls=%async_computation.3 | async-start | bytes 1572864
  48.4 43.5 %copy-start.2 = (bf16[128,256]{1,0:T(8,128)(2,1)S(1)}, bf16[128,256]{1,0:T(8,128)(2,1)}, u32[]{:S(2)}) copy-start(bf16[128,256]{1,0:T(8,128)(2,1)} %param.14) | copy-start | bytes 196612
  190.1 15.4 %collective-permute-start = (bf16[16,3072]{1,0:T(8,128)(2,1)S(1)}, bf16[16,3072]{1,0:T(8,128)(2,1)S(1)}, u32[]{:S(2)}, u32[]{:S(2)}) collective-permute-start(bf16[16,3072]{1,0:T(8,128)(2,1)S(1)} %fusion), channel_id=1, source_target_pairs={{0,32},{32,64},{64,96},{96,128},{128,160},{160,192},{192,224},{224... | collective-permute-start | bytes 294920
  191.4 14.1 %collective-permute-start.1 = (bf16[16,3072]{1,0:T(8,128)(2,1)S(1)}, bf16[16,3072]{1,0:T(8,128)(2,1)S(1)}, u32[]{:S(2)}, u32[]{:S(2)}) collective-permute-start(bf16[16,3072]{1,0:T(8,128)(2,1)S(1)} %fusion), channel_id=1, source_target_pairs={{0,64},{32,96},{64,128},{96,160},{128,192},{160,224},{192,256},{22... | collective-permute-start | bytes 294920
  195.0 11.2 %collective-permute-start.2 = (bf16[16,3072]{1,0:T(8,128)(2,1)S(1)}, bf16[16,3072]{1,0:T(8,128)(2,1)S(1)}, u32[]{:S(2)}, u32[]{:S(2)}) collective-permute-start(bf16[16,3072]{1,0:T(8,128)(2,1)S(1)} %fusion), channel_id=1, source_target_pairs={{0,96},{32,128},{64,160},{96,192},{128,224},{160,256},{192,288},{2... | collective-permute-start | bytes 294920
  199.2 6.4 %collective-permute-start.3 = (bf16[12,3072]{1,0:T(8,128)(2,1)S(1)}, bf16[12,3072]{1,0:T(8,128)(2,1)S(1)}, u32[]{:S(2)}, u32[]{:S(2)}) collective-permute-start(bf16[12,3072]{1,0:T(8,128)(2,1)S(1)} %slice.16), channel_id=1, source_target_pairs={{0,128},{32,160},{64,192},{96,224},{128,256},{160,288},{192,320},{... | collective-permute-start | bytes 221192
  205.6 0.6 copy-start.3
Sparse Core Ops, SparseCore 0:
  10.8 65.3 all-gather.8
  78.2 69.6 all-gather.10
  150.0 74.1 all-gather.6
  228.2 146.4 all-reduce.5
where the time goes:
time: 384 us; the launch traced here: 383 us
  waiting for transfers between devices  246 us (64%)
  blocking collectives  65.5 us (17%)
  other arithmetic  21.9 us (6%)
  between operations  15.3 us (4%)
  matrix products  12.4 us (3%)
  starting transfers between devices  12.3 us (3%)
  local copies, waits for them, and re-layouts  9.14 us (2%)
    unnamed x9, waiting for transfers between devices  147 us
    unnamed x2, blocking collectives  65.5 us
    all_gather x1, waiting for transfers between devices, shards(): lax.all_gather(slot_rows, 'seq', axis=0, tiled=True)  55.7 us
    all_gather x1, waiting for transfers between devices, prefix(): lax.all_gather(part.astype(kind), axis)  26.7 us
    all_gather x1, waiting for transfers between devices, shards(): lax.all_gather(out_weight, 'seq', axis=0, tiled=True)  16.1 us
    select_n x16, other arithmetic, turn(): return jax.tree.map(lambda a, b: jnp.where(reached, a, b), new, before)  14.9 us
    unnamed x5, starting transfers between devices  12.2 us
  transfers between devices with their start and end apart: 8, of which 5 were waited for; matrix products, arithmetic and copies ran while one was open for 18% of the time, Pallas kernels for 0%

commit v1 on v0

--- a/solution.py
+++ b/solution.py
@@ -94,7 +94,9 @@
     slot_rows = jnp.dot(token_pick, normed, preferred_element_type=jnp.float32).astype(jnp.bfloat16)
     gathered_rows, full_weight = (
         lax.all_gather(slot_rows, "seq", axis=0, tiled=True),
-        lax.all_gather(out_weight, "seq", axis=0, tiled=True),
+        jnp.concatenate(
+            lax.all_to_all(jnp.stack([out_weight] * lax.axis_size("seq")), "seq", 0, 0), axis=0
+        ),
     )
     projected = lax.dot_general(
         attn, full_weight, (((1,), (1,)), ((), ())), preferred_element_type=jnp.float32

time: 384 us -> 410 us (1.068)
  blocking collectives: 65.5 us -> 125 us
  waiting for transfers between devices: 246 us -> 195 us
  starting transfers between devices: 12.3 us -> 28.8 us
    unnamed x2, blocking collectives: 65.5 us -> 125 us
    all_gather x1, waiting for transfers between devices: 26.7 us -> 0.02 us  [prefix(): lax.all_gather(part.astype(kind), axis)]
    all_gather x1, waiting for transfers between devices: 55.7 us -> 35.4 us  [shards(): lax.all_gather(slot_rows, 'seq', axis=0, tiled=True)]
    all_gather x1 -> x0, waiting for transfers between devices: 16.1 us -> none  [shards(): lax.all_gather(out_weight, 'seq', axis=0, tiled=True)]
    all_to_all x0 -> x1, starting transfers between devices: none -> 15.9 us  [shards(): lax.all_to_all(jnp.stack([out_weight] * lax.axis_size('seq')), 'seq', 0, 0)]
    unnamed x9 -> x8, waiting for transfers between devices: 147 us -> 160 us
  transfers between devices with their start and end apart: 8 -> 8, of which waited for: 5 -> 3; matrix products, arithmetic and copies ran while one was open for 18% -> 16% of each run, Pallas kernels for 0% -> 0%
where the time goes in v1:
time: 410 us; the launch traced here: 409 us
  waiting for transfers between devices  195 us (48%)
  blocking collectives  125 us (30%)
  starting transfers between devices  28.8 us (7%)
  other arithmetic  20.1 us (5%)
  between operations  15.3 us (4%)
  matrix products  12.4 us (3%)
  local copies, waits for them, and re-layouts  11.3 us (3%)
    unnamed x8, waiting for transfers between devices  160 us
    unnamed x2, blocking collectives  125 us
    all_gather x1, waiting for transfers between devices, shards(): lax.all_gather(slot_rows, 'seq', axis=0, tiled=True)  35.4 us
    all_to_all x1, starting transfers between devices, shards(): lax.all_to_all(jnp.stack([out_weight] * lax.axis_size('seq')), 'seq', 0, 0)  15.9 us
    select_n x16, other arithmetic, turn(): return jax.tree.map(lambda a, b: jnp.where(reached, a, b), new, before)  14.9 us
    unnamed x5, starting transfers between devices  12.8 us
  transfers between devices with their start and end apart: 8, of which 3 were waited for; matrix products, arithmetic and copies ran while one was open for 16% of the time, Pallas kernels for 0%

profile of v1, /device:TPU:1, one launch (start us, length us, event | category | flops | bytes accessed | tf_op | source)
XLA Modules:
  0.0 408.5 jit_solution(419063894703008042)
XLA Ops:
  6.5 1.1 reduce_window_sum.27
  7.9 1.0 copy.68
  8.9 1.7 convolution_convert_fusion.2
  10.6 2.2 stack.2
  12.8 15.9 %all-to-all-start = ((bf16[16,192,256]{2,1,0:T(8,128)(2,1)}), bf16[16,192,256]{2,1,0:T(8,128)(2,1)}, u32[]{:S(2)}, u32[]{:S(2)}) async-start(bf16[16,192,256]{2,1,0:T(8,128)(2,1)} %stack.2), calls=%async_computation | async-start | bytes 3145728 | tf_op jit(solution)/shard_map/all_to_all | solution.py:98
  30.3 1.0 fusion.3
  33.0 92.9 %all-reduce = bf16[32]{0:T(256)(128)(2,1)S(1)} all-reduce(bf16[32]{0:T(256)(128)(2,1)S(1)} %dynamic-update-slice), channel_id=2, replica_groups=mesh['seq'=16,'exp'=32] {'seq'}, use_global_device_ids=true, to_apply=%add | all-reduce | flops 32 | bytes 128
  127.4 15.5 %while.14 = (s32[]{:T(128)}, f32[2,128,128]{2,1,0:T(8,128)S(1)}, s32[]{:T(128)}, bf16[16,2]{1,0:T(8,128)(2,1)S(1)}, bf16[16,2,128,128]{3,2,1,0:T(8,128)(2,1)}, /*index=5*/s32[]{:T(128)}, s32[]{:T(128)}) while((s32[]{:T(128)}, f32[2,128,128]{2,1,0:T(8,128)S(1)}, s32[]{:T(128)}, bf16[16,2]{1,0:T(8,128)(2,1)S(1)}, ...), condition=%wide.region_2.3_spmd.clone, body=%wide.region_1.2_spmd.clone.sunk | while | flops 163846 | bytes 327805 | solution.py:23
  128.4 0.9 fusion.49
  129.4 0.9 fusion.49
  131.3 0.9 fusion.49
  133.2 0.9 fusion.49
  134.2 0.9 fusion.49
  136.2 0.9 fusion.49
  139.1 0.9 fusion.49
  141.0 0.9 fusion.49
  143.5 35.4 %all-gather.8.cloned.1.call-done = bf16[16,12,3072]{2,1,0:T(8,128)(2,1)} async-done(((bf16[1,12,3072]{2,1,0:T(8,128)(2,1)}), bf16[16,12,3072]{2,1,0:T(8,128)(2,1)}) %all-gather.8.cloned.1.call-update) | async-done | bytes 1179664 | tf_op jit(solution)/shard_map/all_gather | solution.py:96
  179.0 2.3 reshape.184
  181.3 4.7 %convolution_convert_fusion = bf16[192,3072]{1,0:T(8,128)(2,1)} fusion(bf16[1,288,3072]{2,1,0:T(8,128)(2,1)S(1)} %copy-done, bf16[192,3072]{1,0:T(8,128)(2,1)} %reshape.184, bf16[1,3072,288]{1,2,0:T(8,128)(2,1)} %param.20), kind=kOutput, calls=%fused_computation.3 | convolution fusion | flops 680343552 | bytes 5898240 | tf_op jit(solution)/shard_map/dot_general | solution.py:108
  186.0 31.9 %fusion = bf16[16,3072]{1,0:T(8,128)(2,1)S(1)} fusion(bf16[192,3072]{1,0:T(8,128)(2,1)} %convolution_convert_fusion), kind=kCustom, calls=%all-reduce-scatter | all-reduce-scatter fusion | flops 786433 | bytes 1280000
  218.0 2.7 collective-permute-start
  220.6 2.1 collective-permute-start.1
  222.8 4.0 collective-permute-start.2
  226.8 4.0 collective-permute-start.3
  230.8 1.6 collective-permute-done.3
  233.0 1.9 concatenate
  235.0 2.1 fusion.34
  237.1 1.8 fusion.2
  238.9 1.3 convert_element_type.97
  240.2 1.3 dynamic-slice.3
  242.1 158.3 %all-reduce.6.cloned.1.call-done = bf16[128,3072]{1,0:T(8,128)(2,1)} async-done(((bf16[128,3072]{1,0:T(8,128)(2,1)}), bf16[128,3072]{1,0:T(8,128)(2,1)}) %all-reduce.6.cloned.1.call-update) | async-done | bytes 786448
  400.5 1.5 add_convert_fusion
  (86 shorter events, 12.6 us)
Async XLA Ops:
  6.5 174.8 %copy-start = (bf16[1,288,3072]{2,1,0:T(8,128)(2,1)S(1)}, bf16[1,288,3072]{2,1,0:T(8,128)(2,1)}, u32[]{:S(2)}) copy-start(bf16[1,288,3072]{2,1,0:T(8,128)(2,1)} %param.21) | copy-start | bytes 5308420
  6.5 120.8 %all-gather.6.cloned.1.call-start = ((), (), s32[]{:S(2)}) async-start(), calls=%async_computation.1 | async-start | bytes 1114112 | tf_op jit(solution)/shard_map/all_gather | solution.py:10
  12.8 16.0 %copy-start.5 = (s32[128,2]{0,1:T(2,128)S(1)}, s32[128,2]{0,1:T(2,128)}, u32[]{:S(2)}) copy-start(s32[128,2]{0,1:T(2,128)} %param.19) | copy-start | bytes 3076
  12.8 17.2 %copy-start.1 = (bf16[128,3072]{1,0:T(8,128)(2,1)S(1)}, bf16[128,3072]{1,0:T(8,128)(2,1)}, u32[]{:S(2)}) copy-start(bf16[128,3072]{1,0:T(8,128)(2,1)} %param.16) | copy-start | bytes 2359300
  12.8 222.2 %all-to-all-start = ((bf16[16,192,256]{2,1,0:T(8,128)(2,1)}), bf16[16,192,256]{2,1,0:T(8,128)(2,1)}, u32[]{:S(2)}, u32[]{:S(2)}) async-start(bf16[16,192,256]{2,1,0:T(8,128)(2,1)} %stack.2), calls=%async_computation | async-start | bytes 3145728 | tf_op jit(solution)/shard_map/all_to_all | solution.py:98
  28.7 2.9 copy-start.6
  28.7 97.3 %copy-start.7 = (bf16[3072,32]{0,1:T(8,128)(2,1)S(1)}, bf16[3072,32]{0,1:T(8,128)(2,1)}, u32[]{:S(2)}) copy-start(bf16[3072,32]{0,1:T(8,128)(2,1)} %param.18) | copy-start | bytes 589828
  28.7 150.3 %all-gather.8.cloned.1.call-start = ((), (), s32[]{:S(2)}) async-start(), calls=%async_computation.2 | async-start | bytes 1671168 | tf_op jit(solution)/shard_map/all_gather | solution.py:96
  29.3 97.2 %copy-start.4 = (bf16[128,256]{1,0:T(8,128)(2,1)S(1)}, bf16[128,256]{1,0:T(8,128)(2,1)}, u32[]{:S(2)}) copy-start(bf16[128,256]{1,0:T(8,128)(2,1)} %param.12) | copy-start | bytes 196612
  31.3 369.2 %all-reduce.6.cloned.1.call-start = ((), (), s32[]{:S(2)}) async-start(), calls=%async_computation.3 | async-start | bytes 1572864
  126.4 16.8 %copy-start.2 = (bf16[128,256]{1,0:T(8,128)(2,1)S(1)}, bf16[128,256]{1,0:T(8,128)(2,1)}, u32[]{:S(2)}) copy-start(bf16[128,256]{1,0:T(8,128)(2,1)} %param.14) | copy-start | bytes 196612
  218.0 14.4 %collective-permute-start = (bf16[16,3072]{1,0:T(8,128)(2,1)S(1)}, bf16[16,3072]{1,0:T(8,128)(2,1)S(1)}, u32[]{:S(2)}, u32[]{:S(2)}) collective-permute-start(bf16[16,3072]{1,0:T(8,128)(2,1)S(1)} %fusion), channel_id=1, source_target_pairs={{0,32},{32,64},{64,96},{96,128},{128,160},{160,192},{192,224},{224... | collective-permute-start | bytes 294920
  220.6 11.8 %collective-permute-start.1 = (bf16[16,3072]{1,0:T(8,128)(2,1)S(1)}, bf16[16,3072]{1,0:T(8,128)(2,1)S(1)}, u32[]{:S(2)}, u32[]{:S(2)}) collective-permute-start(bf16[16,3072]{1,0:T(8,128)(2,1)S(1)} %fusion), channel_id=1, source_target_pairs={{0,64},{32,96},{64,128},{96,160},{128,192},{160,224},{192,256},{22... | collective-permute-start | bytes 294920
  222.8 10.3 %collective-permute-start.2 = (bf16[16,3072]{1,0:T(8,128)(2,1)S(1)}, bf16[16,3072]{1,0:T(8,128)(2,1)S(1)}, u32[]{:S(2)}, u32[]{:S(2)}) collective-permute-start(bf16[16,3072]{1,0:T(8,128)(2,1)S(1)} %fusion), channel_id=1, source_target_pairs={{0,96},{32,128},{64,160},{96,192},{128,224},{160,256},{192,288},{2... | collective-permute-start | bytes 294920
  226.8 5.6 %collective-permute-start.3 = (bf16[12,3072]{1,0:T(8,128)(2,1)S(1)}, bf16[12,3072]{1,0:T(8,128)(2,1)S(1)}, u32[]{:S(2)}, u32[]{:S(2)}) collective-permute-start(bf16[12,3072]{1,0:T(8,128)(2,1)S(1)} %slice.16), channel_id=1, source_target_pairs={{0,128},{32,160},{64,192},{96,224},{128,256},{160,288},{192,320},{... | collective-permute-start | bytes 221192
  232.4 0.6 copy-start.3
Sparse Core Ops, SparseCore 0:
  10.7 102.3 all-gather.5
  115.2 63.7 all-gather.7
  239.0 161.4 all-reduce.5
